TPU v7x, 128 devices: a whole 4x4x4 slice. The times are simulated.
128 devices in a mesh: slab: 8 (over z_lo, x), tile: 16 (over y, z_hi, core).
Axes of the slice: x: 4, y: 4, z: 4 (z_hi: 2, z_lo: 2; z = z_hi * 2 + z_lo), core: 2. Of those that a mesh axis runs over, the one named last changes fastest.
Arguments:
- base_flow: float32 [2, 64, 1024, 128], P(None, 'slab', 'tile'), may hold values from -0.4 to 0.8
- forcing: float32 [64, 4, 1024, 128], P('slab', None, 'tile'), may hold values from -6 to 6
- damping: float32 [1024, 128], P('tile'), may hold values from 0.005 to 0.2
- harmonics: int32 [8], replicated, may hold values from 1 to 31, as said below
Outputs:
- sketch: float32 [8, 2, 4, 1024, 128], P('slab', None, None, 'tile')
Inputs may be any that keep to these rules, and one draw needn't show every extreme that they name: `harmonics`: distinct harmonic indices.
All inputs are finite; a program needn't handle non-finite values.
Results may differ from a plain program's by a relative error of at most 0.0003.
Values sent between devices are 32-bit elements; how exact they have to be, the bound alone decides.
No kernel may reach another device: no remote copies, remote signals or barrier semaphores. Data moves between devices by JAX's collectives and lax.ppermute only.
A program may use at most 64 MiB of HBM per device.

v0:
```python
import math

import jax
import jax.numpy as jnp
from jax import lax
from jax.sharding import PartitionSpec as P

SWEEPS = 2
H = 8


DIFFUSE = 0.15


def with_halo(cells, sides, width):
    for axis, dim in sides:
        count = lax.axis_size(axis)
        ends = count - 1
        head = lax.slice_in_dim(cells, 0, width, axis=dim)
        tail = lax.slice_in_dim(cells, cells.shape[dim] - width, cells.shape[dim], axis=dim)
        cells = jnp.concatenate(
            [
                lax.ppermute(tail, axis, [(i, (i + 1) % count) for i in range(ends)]),
                cells,
                lax.ppermute(head, axis, [((i + 1) % count, i) for i in range(ends)]),
            ],
            axis=dim,
        )
    return cells


def passed_along(block, axis, distance):
    devices = range(lax.axis_size(axis))
    route = [((i - distance) % len(devices), i) for i in devices]
    return lax.ppermute(block, axis, route)


def laplace(padded, center):
    return (
        padded[..., 2:, 1:-1]
        + padded[..., :-2, 1:-1]
        + padded[..., 1:-1, 2:]
        + padded[..., 1:-1, :-2]
        - 4.0 * center
    )


def pad_columns(field):
    widths = [(0, 0)] * (field.ndim - 1) + [(1, 1)]
    return jnp.pad(field, widths)


def forward_inner(extended, speed_x, speed_y, damping, source):
    padded = pad_columns(extended)
    center = extended[..., 1:-1, :]
    grad_x = 0.5 * (padded[..., 2:, 1:-1] - padded[..., :-2, 1:-1])
    grad_y = 0.5 * (padded[..., 1:-1, 2:] - padded[..., 1:-1, :-2])
    return (
        source
        - (speed_x * grad_x + speed_y * grad_y)
        + DIFFUSE * laplace(padded, center)
        - damping * center
    )


def adjoint_inner(extended, flux_x, flux_y, damping, source):
    padded = pad_columns(extended)
    center = extended[..., 1:-1, :]
    padded_x = pad_columns(flux_x)
    padded_y = pad_columns(flux_y)
    div_x = 0.5 * (padded_x[..., 2:, 1:-1] - padded_x[..., :-2, 1:-1])
    div_y = 0.5 * (padded_y[..., 1:-1, 2:] - padded_y[..., 1:-1, :-2])
    return source + div_x + div_y + DIFFUSE * laplace(padded, center) - damping * center


def forward_rate(state, speed_x, speed_y, damping, source):
    extended = with_halo(state, (("tile", 1),), 1)
    return forward_inner(extended, speed_x, speed_y, damping, source)


def adjoint_rate(state, speed_x, speed_y, damping, source):
    stacked = jnp.stack([state, speed_x * state, speed_y * state])
    extended = with_halo(stacked, (("tile", 2),), 1)
    return adjoint_inner(extended[0], extended[1], extended[2], damping, source)


def coefficient_table(chosen, phase, periods):
    turns = chosen[:, None] * phase[None, :] % periods
    angle = 2.0 * math.pi / periods * turns.astype(jnp.float32)
    table = jnp.stack([jnp.cos(angle), -jnp.sin(angle)], axis=1) * (1.0 / math.sqrt(periods))
    return table.reshape(2 * chosen.shape[0], phase.shape[0])


def on_device(base_flow, forcing, damping, harmonics):
    steps = forcing.shape[0]
    count_f, rows, columns = (forcing.shape[1], forcing.shape[2], forcing.shape[3])
    slabs = lax.axis_size("slab")
    periods = steps * slabs
    start = jnp.zeros((count_f, rows, columns), jnp.float32)
    for sweep in range(SWEEPS):
        state = start
        record = []
        for step in range(steps):
            record.append(state)
            speed_x = base_flow[0, step]
            speed_y = base_flow[1, step]
            first = forward_rate(state, speed_x, speed_y, damping, forcing[step])
            second = forward_rate(state + first, speed_x, speed_y, damping, forcing[step])
            state = state + 0.5 * (first + second)
        if sweep + 1 < SWEEPS:
            start = passed_along(state, "slab", 1)
    response = record
    start = jnp.zeros((count_f, rows, columns), jnp.float32)
    for sweep in range(SWEEPS):
        state = start
        record = [None] * steps
        for step in range(steps - 1, -1, -1):
            speed_x = base_flow[0, step]
            speed_y = base_flow[1, step]
            first = adjoint_rate(state, speed_x, speed_y, damping, response[step])
            second = adjoint_rate(state + first, speed_x, speed_y, damping, response[step])
            state = state + 0.5 * (first + second)
            record[step] = state
        if sweep + 1 < SWEEPS:
            start = passed_along(state, "slab", -1)
    adjoint = jnp.stack(record, axis=0)
    phase = lax.axis_index("slab") * steps + jnp.arange(steps, dtype=jnp.int32)
    flat = adjoint.reshape(steps, count_f * rows * columns)
    table = coefficient_table(harmonics, phase, periods)
    terms = jnp.dot(table, flat, precision=lax.Precision.HIGHEST)
    return lax.psum_scatter(
        terms.reshape(H // slabs * lax.axis_size("slab"), 2, count_f, rows, columns),
        "slab",
        scatter_dimension=0,
        tiled=True,
    )


def solution(mesh):
    return jax.shard_map(
        on_device,
        mesh=mesh,
        in_specs=(
            P(None, "slab", "tile", None),
            P("slab", None, "tile", None),
            P("tile", None),
            P(),
        ),
        out_specs=P("slab", None, None, "tile", None),
        check_vma=False,
    )
```

profile of v0, /device:TPU:16, one launch (start us, length us, event | category | flops | bytes accessed | tf_op | source)
XLA Modules:
  0.0 684.9 jit_solution(13247067131885312705)
XLA Ops:
  8.6 6.0 collective-permute-start
  174.1 6.5 collective-permute-done.32
  182.6 6.0 collective-permute-start.33
  192.2 6.0 collective-permute-start.35
  201.9 6.0 collective-permute-start.37
  211.5 6.0 collective-permute-start.39
  221.3 6.0 collective-permute-start.41
  230.9 6.0 collective-permute-start.43
  240.6 6.0 collective-permute-start.45
  250.2 6.0 collective-permute-start.47
  259.9 6.2 collective-permute-start.49
  269.5 6.0 collective-permute-start.51
  279.3 6.0 collective-permute-start.53
  287.3 6.0 collective-permute-start.62
  295.7 6.0 collective-permute-start.55
  305.4 6.0 collective-permute-start.57
  315.0 6.0 collective-permute-start.59
  324.9 6.0 collective-permute-start.64
  334.6 6.0 collective-permute-start.66
  344.3 6.0 collective-permute-start.68
  353.9 6.0 collective-permute-start.70
  363.6 6.0 collective-permute-start.72
  373.3 6.0 collective-permute-start.74
  383.0 6.0 collective-permute-start.76
  392.6 6.0 collective-permute-start.78
  484.7 6.0 collective-permute-start.97
  494.4 6.3 collective-permute-start.99
  504.0 6.0 collective-permute-start.101
  523.4 6.0 collective-permute-start.105
  581.4 6.0 collective-permute-start.117
  591.0 6.0 collective-permute-start.119
  632.9 45.2 %reduce-scatter.2.cloned.1.call-done = f32[1,2,4,64,128]{4,3,2,1,0:T(8,128)} async-done(((f32[8,2,4,64,128]{4,3,2,1,0:T(8,128)}), f32[1,2,4,64,128]{4,3,2,1,0:T(8,128)}) %reduce-scatter.2.cloned.1.call-update) | async-done | bytes 262160 | tf_op jit(solution)/shard_map/reduce_scatter | solution.py:131
  (491 shorter events, 435.0 us)
Async XLA Ops:
  6.5 671.5 %reduce-scatter.2.cloned.1.call-start = ((), (), s32[]{:S(2)}) async-start(), calls=%async_computation.1 | async-start | bytes 2359296 | tf_op jit(solution)/shard_map/reduce_scatter | solution.py:131
  6.5 9.3 %collective-permute-start.1 = (f32[4,1,128]{2,1,0:T(1,128)S(1)}, f32[4,1,128]{2,1,0:T(1,128)S(1)}, u32[]{:S(2)}, u32[]{:S(2)}) collective-permute-start(f32[4,1,128]{2,1,0:T(1,128)S(1)} %broadcast.477), channel_id=1, source_target_pairs={{0,1},{1,2},{2,3},{3,4},{4,5},{5,6},{6,7},{7,8},{8,9},{9,10},{10,1... | collective-permute-start | bytes 6152 | tf_op jit(solution)/shard_map/ppermute | solution.py:23
  26.7 8.0 %collective-permute-start.5 = (f32[4,1,128]{2,1,0:T(1,128)S(1)}, f32[4,1,128]{2,1,0:T(1,128)S(1)}, u32[]{:S(2)}, u32[]{:S(2)}) collective-permute-start(f32[4,1,128]{2,1,0:T(1,128)S(1)} %get-tuple-element.352), channel_id=1, source_target_pairs={{0,1},{1,2},{2,3},{3,4},{4,5},{5,6},{6,7},{7,8},{8,9},{9,10},{10,1... | collective-permute-start | bytes 6152 | tf_op jit(solution)/shard_map/ppermute | solution.py:23
  140.9 8.0 %collective-permute-start.27 = (f32[4,1,128]{2,1,0:T(1,128)S(1)}, f32[4,1,128]{2,1,0:T(1,128)S(1)}, u32[]{:S(2)}, u32[]{:S(2)}) collective-permute-start(f32[4,1,128]{2,1,0:T(1,128)S(1)} %get-tuple-element.330), channel_id=1, source_target_pairs={{0,1},{1,2},{2,3},{3,4},{4,5},{5,6},{6,7},{7,8},{8,9},{9,10},{10,1... | collective-permute-start | bytes 6152 | tf_op jit(solution)/shard_map/ppermute | solution.py:23
  162.0 8.0 %collective-permute-start.31 = (f32[4,1,128]{2,1,0:T(1,128)S(1)}, f32[4,1,128]{2,1,0:T(1,128)S(1)}, u32[]{:S(2)}, u32[]{:S(2)}) collective-permute-start(f32[4,1,128]{2,1,0:T(1,128)S(1)} %get-tuple-element.326), channel_id=1, source_target_pairs={{0,1},{1,2},{2,3},{3,4},{4,5},{5,6},{6,7},{7,8},{8,9},{9,10},{10,1... | collective-permute-start | bytes 6152 | tf_op jit(solution)/shard_map/ppermute | solution.py:23
  172.6 8.1 %collective-permute-start.32 = (f32[4,64,128]{2,1,0:T(8,128)S(1)}, f32[4,64,128]{2,1,0:T(8,128)S(1)}, u32[]{:S(2)}, u32[]{:S(2)}) collective-permute-start(f32[4,64,128]{2,1,0:T(8,128)S(1)} %fusion.405), channel_id=1, source_target_pairs={{112,0},{0,16},{16,32},{32,48},{48,64},{64,80},{80,96},{96,112},{1... | collective-permute-start | bytes 393224 | tf_op jit(solution)/shard_map/ppermute | solution.py:35
  190.3 8.0 %collective-permute-start.36 = (f32[4,1,128]{2,1,0:T(1,128)S(1)}, f32[4,1,128]{2,1,0:T(1,128)S(1)}, u32[]{:S(2)}, u32[]{:S(2)}) collective-permute-start(f32[4,1,128]{2,1,0:T(1,128)S(1)} %get-tuple-element.322), channel_id=1, source_target_pairs={{0,1},{1,2},{2,3},{3,4},{4,5},{5,6},{6,7},{7,8},{8,9},{9,10},{10,1... | collective-permute-start | bytes 6152 | tf_op jit(solution)/shard_map/ppermute | solution.py:23
  200.0 8.0 %collective-permute-start.38 = (f32[4,1,128]{2,1,0:T(1,128)S(1)}, f32[4,1,128]{2,1,0:T(1,128)S(1)}, u32[]{:S(2)}, u32[]{:S(2)}) collective-permute-start(f32[4,1,128]{2,1,0:T(1,128)S(1)} %get-tuple-element.320), channel_id=1, source_target_pairs={{0,1},{1,2},{2,3},{3,4},{4,5},{5,6},{6,7},{7,8},{8,9},{9,10},{10,1... | collective-permute-start | bytes 6152 | tf_op jit(solution)/shard_map/ppermute | solution.py:23
  219.3 8.0 %collective-permute-start.42 = (f32[4,1,128]{2,1,0:T(1,128)S(1)}, f32[4,1,128]{2,1,0:T(1,128)S(1)}, u32[]{:S(2)}, u32[]{:S(2)}) collective-permute-start(f32[4,1,128]{2,1,0:T(1,128)S(1)} %get-tuple-element.316), channel_id=1, source_target_pairs={{0,1},{1,2},{2,3},{3,4},{4,5},{5,6},{6,7},{7,8},{8,9},{9,10},{10,1... | collective-permute-start | bytes 6152 | tf_op jit(solution)/shard_map/ppermute | solution.py:23
  238.7 8.0 %collective-permute-start.46 = (f32[4,1,128]{2,1,0:T(1,128)S(1)}, f32[4,1,128]{2,1,0:T(1,128)S(1)}, u32[]{:S(2)}, u32[]{:S(2)}) collective-permute-start(f32[4,1,128]{2,1,0:T(1,128)S(1)} %get-tuple-element.312), channel_id=1, source_target_pairs={{0,1},{1,2},{2,3},{3,4},{4,5},{5,6},{6,7},{7,8},{8,9},{9,10},{10,1... | collective-permute-start | bytes 6152 | tf_op jit(solution)/shard_map/ppermute | solution.py:23
  258.0 8.2 %collective-permute-start.50 = (f32[4,1,128]{2,1,0:T(1,128)S(1)}, f32[4,1,128]{2,1,0:T(1,128)S(1)}, u32[]{:S(2)}, u32[]{:S(2)}) collective-permute-start(f32[4,1,128]{2,1,0:T(1,128)S(1)} %get-tuple-element.308), channel_id=1, source_target_pairs={{0,1},{1,2},{2,3},{3,4},{4,5},{5,6},{6,7},{7,8},{8,9},{9,10},{10,1... | collective-permute-start | bytes 6152 | tf_op jit(solution)/shard_map/ppermute | solution.py:23
  267.6 8.0 %collective-permute-start.52 = (f32[4,1,128]{2,1,0:T(1,128)S(1)}, f32[4,1,128]{2,1,0:T(1,128)S(1)}, u32[]{:S(2)}, u32[]{:S(2)}) collective-permute-start(f32[4,1,128]{2,1,0:T(1,128)S(1)} %get-tuple-element.306), channel_id=1, source_target_pairs={{0,1},{1,2},{2,3},{3,4},{4,5},{5,6},{6,7},{7,8},{8,9},{9,10},{10,1... | collective-permute-start | bytes 6152 | tf_op jit(solution)/shard_map/ppermute | solution.py:23
  277.4 16.0 %collective-permute-start.54 = (f32[4,1,128]{2,1,0:T(1,128)S(1)}, f32[4,1,128]{2,1,0:T(1,128)S(1)}, u32[]{:S(2)}, u32[]{:S(2)}) collective-permute-start(f32[4,1,128]{2,1,0:T(1,128)S(1)} %get-tuple-element.304), channel_id=1, source_target_pairs={{0,1},{1,2},{2,3},{3,4},{4,5},{5,6},{6,7},{7,8},{8,9},{9,10},{10,1... | collective-permute-start | bytes 6152 | tf_op jit(solution)/shard_map/ppermute | solution.py:23
  279.3 14.1 %collective-permute-start.53 = (f32[4,1,128]{2,1,0:T(1,128)S(1)}, f32[4,1,128]{2,1,0:T(1,128)S(1)}, u32[]{:S(2)}, u32[]{:S(2)}) collective-permute-start(f32[4,1,128]{2,1,0:T(1,128)S(1)} %get-tuple-element.305), channel_id=1, source_target_pairs={{1,0},{2,1},{3,2},{4,3},{5,4},{6,5},{7,6},{8,7},{9,8},{10,9},{11,1... | collective-permute-start | bytes 6152 | tf_op jit(solution)/shard_map/ppermute | solution.py:25
  285.4 26.1 %collective-permute-start.61 = (f32[3,4,1,128]{3,2,1,0:T(1,128)S(1)}, f32[3,4,1,128]{3,2,1,0:T(1,128)S(1)}, u32[]{:S(2)}, u32[]{:S(2)}) collective-permute-start(f32[3,4,1,128]{3,2,1,0:T(1,128)S(1)} %get-tuple-element.262), channel_id=1, source_target_pairs={{0,1},{1,2},{2,3},{3,4},{4,5},{5,6},{6,7},{7,8},{8,9},{9,10},{10,1... | collective-permute-start | bytes 18440 | tf_op jit(solution)/shard_map/ppermute | solution.py:23
  287.3 24.1 %collective-permute-start.62 = (f32[3,4,1,128]{3,2,1,0:T(1,128)S(1)}, f32[3,4,1,128]{3,2,1,0:T(1,128)S(1)}, u32[]{:S(2)}, u32[]{:S(2)}) collective-permute-start(f32[3,4,1,128]{3,2,1,0:T(1,128)S(1)} %get-tuple-element.263), channel_id=1, source_target_pairs={{1,0},{2,1},{3,2},{4,3},{5,4},{6,5},{7,6},{8,7},{9,8},{10,9},{11,1... | collective-permute-start | bytes 18440 | tf_op jit(solution)/shard_map/ppermute | solution.py:25
  293.8 8.0 %collective-permute-start.56 = (f32[4,1,128]{2,1,0:T(1,128)S(1)}, f32[4,1,128]{2,1,0:T(1,128)S(1)}, u32[]{:S(2)}, u32[]{:S(2)}) collective-permute-start(f32[4,1,128]{2,1,0:T(1,128)S(1)} %get-tuple-element.302), channel_id=1, source_target_pairs={{0,1},{1,2},{2,3},{3,4},{4,5},{5,6},{6,7},{7,8},{8,9},{9,10},{10,1... | collective-permute-start | bytes 6152 | tf_op jit(solution)/shard_map/ppermute | solution.py:23
  303.5 8.1 %collective-permute-start.58 = (f32[4,1,128]{2,1,0:T(1,128)S(1)}, f32[4,1,128]{2,1,0:T(1,128)S(1)}, u32[]{:S(2)}, u32[]{:S(2)}) collective-permute-start(f32[4,1,128]{2,1,0:T(1,128)S(1)} %get-tuple-element.300), channel_id=1, source_target_pairs={{0,1},{1,2},{2,3},{3,4},{4,5},{5,6},{6,7},{7,8},{8,9},{9,10},{10,1... | collective-permute-start | bytes 6152 | tf_op jit(solution)/shard_map/ppermute | solution.py:23
  313.1 8.0 %collective-permute-start.60 = (f32[4,1,128]{2,1,0:T(1,128)S(1)}, f32[4,1,128]{2,1,0:T(1,128)S(1)}, u32[]{:S(2)}, u32[]{:S(2)}) collective-permute-start(f32[4,1,128]{2,1,0:T(1,128)S(1)} %get-tuple-element.298), channel_id=1, source_target_pairs={{0,1},{1,2},{2,3},{3,4},{4,5},{5,6},{6,7},{7,8},{8,9},{9,10},{10,1... | collective-permute-start | bytes 6152 | tf_op jit(solution)/shard_map/ppermute | solution.py:23
  323.0 8.0 %collective-permute-start.63 = (f32[3,4,1,128]{3,2,1,0:T(1,128)S(1)}, f32[3,4,1,128]{3,2,1,0:T(1,128)S(1)}, u32[]{:S(2)}, u32[]{:S(2)}) collective-permute-start(f32[3,4,1,128]{3,2,1,0:T(1,128)S(1)} %get-tuple-element.260), channel_id=1, source_target_pairs={{0,1},{1,2},{2,3},{3,4},{4,5},{5,6},{6,7},{7,8},{8,9},{9,10},{10,1... | collective-permute-start | bytes 18440 | tf_op jit(solution)/shard_map/ppermute | solution.py:23
  332.7 8.0 %collective-permute-start.65 = (f32[3,4,1,128]{3,2,1,0:T(1,128)S(1)}, f32[3,4,1,128]{3,2,1,0:T(1,128)S(1)}, u32[]{:S(2)}, u32[]{:S(2)}) collective-permute-start(f32[3,4,1,128]{3,2,1,0:T(1,128)S(1)} %get-tuple-element.258), channel_id=1, source_target_pairs={{0,1},{1,2},{2,3},{3,4},{4,5},{5,6},{6,7},{7,8},{8,9},{9,10},{10,1... | collective-permute-start | bytes 18440 | tf_op jit(solution)/shard_map/ppermute | solution.py:23
  371.4 8.0 %collective-permute-start.73 = (f32[3,4,1,128]{3,2,1,0:T(1,128)S(1)}, f32[3,4,1,128]{3,2,1,0:T(1,128)S(1)}, u32[]{:S(2)}, u32[]{:S(2)}) collective-permute-start(f32[3,4,1,128]{3,2,1,0:T(1,128)S(1)} %get-tuple-element.250), channel_id=1, source_target_pairs={{0,1},{1,2},{2,3},{3,4},{4,5},{5,6},{6,7},{7,8},{8,9},{9,10},{10,1... | collective-permute-start | bytes 18440 | tf_op jit(solution)/shard_map/ppermute | solution.py:23
  381.0 8.0 %collective-permute-start.75 = (f32[3,4,1,128]{3,2,1,0:T(1,128)S(1)}, f32[3,4,1,128]{3,2,1,0:T(1,128)S(1)}, u32[]{:S(2)}, u32[]{:S(2)}) collective-permute-start(f32[3,4,1,128]{3,2,1,0:T(1,128)S(1)} %get-tuple-element.248), channel_id=1, source_target_pairs={{0,1},{1,2},{2,3},{3,4},{4,5},{5,6},{6,7},{7,8},{8,9},{9,10},{10,1... | collective-permute-start | bytes 18440 | tf_op jit(solution)/shard_map/ppermute | solution.py:23
  390.7 8.0 %collective-permute-start.77 = (f32[3,4,1,128]{3,2,1,0:T(1,128)S(1)}, f32[3,4,1,128]{3,2,1,0:T(1,128)S(1)}, u32[]{:S(2)}, u32[]{:S(2)}) collective-permute-start(f32[3,4,1,128]{3,2,1,0:T(1,128)S(1)} %get-tuple-element.246), channel_id=1, source_target_pairs={{0,1},{1,2},{2,3},{3,4},{4,5},{5,6},{6,7},{7,8},{8,9},{9,10},{10,1... | collective-permute-start | bytes 18440 | tf_op jit(solution)/shard_map/ppermute | solution.py:23
  400.4 8.0 %collective-permute-start.79 = (f32[3,4,1,128]{3,2,1,0:T(1,128)S(1)}, f32[3,4,1,128]{3,2,1,0:T(1,128)S(1)}, u32[]{:S(2)}, u32[]{:S(2)}) collective-permute-start(f32[3,4,1,128]{3,2,1,0:T(1,128)S(1)} %get-tuple-element.244), channel_id=1, source_target_pairs={{0,1},{1,2},{2,3},{3,4},{4,5},{5,6},{6,7},{7,8},{8,9},{9,10},{10,1... | collective-permute-start | bytes 18440 | tf_op jit(solution)/shard_map/ppermute | solution.py:23
  429.4 8.0 %collective-permute-start.85 = (f32[3,4,1,128]{3,2,1,0:T(1,128)S(1)}, f32[3,4,1,128]{3,2,1,0:T(1,128)S(1)}, u32[]{:S(2)}, u32[]{:S(2)}) collective-permute-start(f32[3,4,1,128]{3,2,1,0:T(1,128)S(1)} %get-tuple-element.238), channel_id=1, source_target_pairs={{0,1},{1,2},{2,3},{3,4},{4,5},{5,6},{6,7},{7,8},{8,9},{9,10},{10,1... | collective-permute-start | bytes 18440 | tf_op jit(solution)/shard_map/ppermute | solution.py:23
  439.1 8.0 %collective-permute-start.87 = (f32[3,4,1,128]{3,2,1,0:T(1,128)S(1)}, f32[3,4,1,128]{3,2,1,0:T(1,128)S(1)}, u32[]{:S(2)}, u32[]{:S(2)}) collective-permute-start(f32[3,4,1,128]{3,2,1,0:T(1,128)S(1)} %get-tuple-element.236), channel_id=1, source_target_pairs={{0,1},{1,2},{2,3},{3,4},{4,5},{5,6},{6,7},{7,8},{8,9},{9,10},{10,1... | collective-permute-start | bytes 18440 | tf_op jit(solution)/shard_map/ppermute | solution.py:23
  448.7 8.0 %collective-permute-start.89 = (f32[3,4,1,128]{3,2,1,0:T(1,128)S(1)}, f32[3,4,1,128]{3,2,1,0:T(1,128)S(1)}, u32[]{:S(2)}, u32[]{:S(2)}) collective-permute-start(f32[3,4,1,128]{3,2,1,0:T(1,128)S(1)} %get-tuple-element.234), channel_id=1, source_target_pairs={{0,1},{1,2},{2,3},{3,4},{4,5},{5,6},{6,7},{7,8},{8,9},{9,10},{10,1... | collective-permute-start | bytes 18440 | tf_op jit(solution)/shard_map/ppermute | solution.py:23
  492.4 8.2 %collective-permute-start.98 = (f32[3,4,1,128]{3,2,1,0:T(1,128)S(1)}, f32[3,4,1,128]{3,2,1,0:T(1,128)S(1)}, u32[]{:S(2)}, u32[]{:S(2)}) collective-permute-start(f32[3,4,1,128]{3,2,1,0:T(1,128)S(1)} %get-tuple-element.226), channel_id=1, source_target_pairs={{0,1},{1,2},{2,3},{3,4},{4,5},{5,6},{6,7},{7,8},{8,9},{9,10},{10,1... | collective-permute-start | bytes 18440 | tf_op jit(solution)/shard_map/ppermute | solution.py:23
  598.8 8.0 %collective-permute-start.120 = (f32[3,4,1,128]{3,2,1,0:T(1,128)S(1)}, f32[3,4,1,128]{3,2,1,0:T(1,128)S(1)}, u32[]{:S(2)}, u32[]{:S(2)}) collective-permute-start(f32[3,4,1,128]{3,2,1,0:T(1,128)S(1)} %get-tuple-element.204), channel_id=1, source_target_pairs={{0,1},{1,2},{2,3},{3,4},{4,5},{5,6},{6,7},{7,8},{8,9},{9,10},{10,1... | collective-permute-start | bytes 18440 | tf_op jit(solution)/shard_map/ppermute | solution.py:23
  608.5 8.0 %collective-permute-start.122 = (f32[3,4,1,128]{3,2,1,0:T(1,128)S(1)}, f32[3,4,1,128]{3,2,1,0:T(1,128)S(1)}, u32[]{:S(2)}, u32[]{:S(2)}) collective-permute-start(f32[3,4,1,128]{3,2,1,0:T(1,128)S(1)} %get-tuple-element.202), channel_id=1, source_target_pairs={{0,1},{1,2},{2,3},{3,4},{4,5},{5,6},{6,7},{7,8},{8,9},{9,10},{10,1... | collective-permute-start | bytes 18440 | tf_op jit(solution)/shard_map/ppermute | solution.py:23
  618.1 8.1 %collective-permute-start.124 = (f32[3,4,1,128]{3,2,1,0:T(1,128)S(1)}, f32[3,4,1,128]{3,2,1,0:T(1,128)S(1)}, u32[]{:S(2)}, u32[]{:S(2)}) collective-permute-start(f32[3,4,1,128]{3,2,1,0:T(1,128)S(1)} %get-tuple-element.200), channel_id=1, source_target_pairs={{0,1},{1,2},{2,3},{3,4},{4,5},{5,6},{6,7},{7,8},{8,9},{9,10},{10,1... | collective-permute-start | bytes 18440 | tf_op jit(solution)/shard_map/ppermute | solution.py:23
  (99 other events, 792.6 us)
Sparse Core Ops, SparseCore 0:
  633.0 45.0 reduce-scatter.1
where the time goes:
time: 689 us; the launch traced here: 685 us
  starting transfers between devices  498 us (72%)
  waiting for transfers between devices  131 us (19%)
  other arithmetic  33.3 us (5%)
  between operations  16.4 us (2%)
    ppermute x62, starting transfers between devices, with_halo(): lax.ppermute(head, axis, [((i + 1) % count, i) for i in range(ends)])  366 us
    ppermute x62, starting transfers between devices, with_halo(): lax.ppermute(tail, axis, [(i, (i + 1) % count) for i in range(ends)])  129 us
    ppermute x62, waiting for transfers between devices, with_halo(): lax.ppermute(head, axis, [((i + 1) % count, i) for i in range(ends)])  75.9 us
    reduce_scatter x1, waiting for transfers between devices, on_device(): lax.psum_scatter(terms.reshape(H // slabs * lax.axis_size('slab'), 2, cou...  45.2 us
  transfers between devices with their start and end apart: 127, of which 63 were waited for; matrix products, arithmetic and copies ran while one was open for 0% of the time, Pallas kernels for 0%

commit v1 on v0

v1 whole, which is shorter than its diff:
```python
import math

import jax
import jax.numpy as jnp
from jax import lax
from jax.sharding import PartitionSpec as P

SWEEPS = 2
H = 8


DIFFUSE = 0.15


def passed_along(block, axis, distance):
    devices = range(lax.axis_size(axis))
    route = [((i - distance) % len(devices), i) for i in devices]
    return lax.ppermute(block, axis, route)


def with_neighbours(block, axis, dim):
    count = lax.axis_size(axis)
    before = lax.ppermute(block, axis, [(i, i + 1) for i in range(count - 1)])
    after = lax.ppermute(block, axis, [(i + 1, i) for i in range(count - 1)])
    return jnp.concatenate([before, block, after], axis=dim)


def pad_grid(field):
    widths = [(0, 0)] * (field.ndim - 2) + [(1, 1), (1, 1)]
    return jnp.pad(field, widths)


def laplace(padded, center):
    return (
        padded[..., 2:, 1:-1]
        + padded[..., :-2, 1:-1]
        + padded[..., 1:-1, 2:]
        + padded[..., 1:-1, :-2]
        - 4.0 * center
    )


def forward_rate(state, speed_x, speed_y, damping, source, mask):
    padded = pad_grid(state)
    grad_x = 0.5 * (padded[..., 2:, 1:-1] - padded[..., :-2, 1:-1])
    grad_y = 0.5 * (padded[..., 1:-1, 2:] - padded[..., 1:-1, :-2])
    rate = source - (speed_x * grad_x + speed_y * grad_y) + DIFFUSE * laplace(padded, state) - damping * state
    return rate * mask


def adjoint_rate(state, speed_x, speed_y, damping, source, mask):
    padded = pad_grid(state)
    flux_x = pad_grid(speed_x * state)
    flux_y = pad_grid(speed_y * state)
    div_x = 0.5 * (flux_x[..., 2:, 1:-1] - flux_x[..., :-2, 1:-1])
    div_y = 0.5 * (flux_y[..., 1:-1, 2:] - flux_y[..., 1:-1, :-2])
    rate = source + div_x + div_y + DIFFUSE * laplace(padded, state) - damping * state
    return rate * mask


def coefficient_table(chosen, phase, periods):
    turns = chosen[:, None] * phase[None, :] % periods
    angle = 2.0 * math.pi / periods * turns.astype(jnp.float32)
    table = jnp.stack([jnp.cos(angle), -jnp.sin(angle)], axis=1) * (1.0 / math.sqrt(periods))
    return table.reshape(2 * chosen.shape[0], phase.shape[0])


def on_device(base_flow, forcing, damping, harmonics):
    steps = forcing.shape[0]
    count_f, rows, columns = (forcing.shape[1], forcing.shape[2], forcing.shape[3])
    slabs = lax.axis_size("slab")
    tiles = lax.axis_size("tile")
    periods = steps * slabs

    packed = jnp.concatenate(
        [base_flow.reshape(2 * steps, rows, columns), forcing.reshape(steps * count_f, rows, columns), damping[None]],
        axis=0,
    )
    wide = with_neighbours(packed, "tile", 1)
    ext = 3 * rows
    flow = wide[: 2 * steps].reshape(2, steps, ext, columns)
    drive = wide[2 * steps : 2 * steps + steps * count_f].reshape(steps, count_f, ext, columns)
    damp = wide[-1]
    row = lax.axis_index("tile") * rows - rows + jnp.arange(ext, dtype=jnp.int32)
    mask = ((row >= 0) & (row < tiles * rows)).astype(jnp.float32)[:, None]

    start = jnp.zeros((count_f, ext, columns), jnp.float32)
    for sweep in range(SWEEPS):
        state = start
        record = []
        for step in range(steps):
            record.append(state)
            speed_x = flow[0, step]
            speed_y = flow[1, step]
            first = forward_rate(state, speed_x, speed_y, damp, drive[step], mask)
            second = forward_rate(state + first, speed_x, speed_y, damp, drive[step], mask)
            state = state + 0.5 * (first + second)
        if sweep + 1 < SWEEPS:
            start = passed_along(state, "slab", 1)
    response = record
    start = jnp.zeros((count_f, ext, columns), jnp.float32)
    for sweep in range(SWEEPS):
        state = start
        record = [None] * steps
        for step in range(steps - 1, -1, -1):
            speed_x = flow[0, step]
            speed_y = flow[1, step]
            first = adjoint_rate(state, speed_x, speed_y, damp, response[step], mask)
            second = adjoint_rate(state + first, speed_x, speed_y, damp, response[step], mask)
            state = state + 0.5 * (first + second)
            record[step] = state
        if sweep + 1 < SWEEPS:
            start = passed_along(state, "slab", -1)
    adjoint = jnp.stack(record, axis=0)[:, :, rows : 2 * rows]
    phase = lax.axis_index("slab") * steps + jnp.arange(steps, dtype=jnp.int32)
    flat = adjoint.reshape(steps, count_f * rows * columns)
    table = coefficient_table(harmonics, phase, periods)
    terms = jnp.dot(table, flat, precision=lax.Precision.HIGHEST)
    return lax.psum_scatter(
        terms.reshape(H // slabs * lax.axis_size("slab"), 2, count_f, rows, columns),
        "slab",
        scatter_dimension=0,
        tiled=True,
    )


def solution(mesh):
    return jax.shard_map(
        on_device,
        mesh=mesh,
        in_specs=(
            P(None, "slab", "tile", None),
            P("slab", None, "tile", None),
            P("tile", None),
            P(),
        ),
        out_specs=P("slab", None, None, "tile", None),
        check_vma=False,
    )
```

time: 689 us -> 182 us (0.26)
  starting transfers between devices: 498 us -> 9.94 us
  waiting for transfers between devices: 131 us -> 95.7 us
  other arithmetic: 33.3 us -> 52.3 us
    ppermute x124 -> x2, starting transfers between devices: 494 us -> 7.02 us  [the longest x1 5.1 us: with_neighbours(): after = lax.ppermute(block, axis, [(i + 1, i) for i in range(count - 1)])]
    ppermute x124 -> x2, waiting for transfers between devices: 76 us -> 22.7 us  [the longest x1 16.5 us: with_neighbours(): after = lax.ppermute(block, axis, [(i + 1, i) for i in range(count - 1)])]
    mul x1 -> x66, other arithmetic: 1.08 us -> 31.9 us  [the longest x29 29.2 us: adjoint_rate(): flux_y = pad_grid(speed_y * state)]
    reduce_scatter x1, waiting for transfers between devices: 45.2 us -> 58.1 us  [on_device(): lax.psum_scatter(terms.reshape(H // slabs * lax.axis_size('slab'), 2, cou...]
    another operation x61 -> x0, other arithmetic: 7.41 us -> none  [adjoint_rate(): stacked = jnp.stack([state, speed_x * state, speed_y * state])]
  transfers between devices with their start and end apart: 127 -> 5, of which waited for: 63 -> 5; matrix products, arithmetic and copies ran while one was open for 0% -> 0% of each run, Pallas kernels for 0% -> 0%
where the time goes in v1:
time: 182 us; the launch traced here: 180 us
  waiting for transfers between devices  95.7 us (53%)
  other arithmetic  52.3 us (29%)
  between operations  14.7 us (8%)
  starting transfers between devices  9.94 us (5%)
  local copies, waits for them, and re-layouts  5.94 us (3%)
    reduce_scatter x1, waiting for transfers between devices, on_device(): lax.psum_scatter(terms.reshape(H // slabs * lax.axis_size('slab'), 2, cou...  58.1 us
    mul x29, other arithmetic, adjoint_rate(): flux_y = pad_grid(speed_y * state)  29.2 us
    ppermute x1, waiting for transfers between devices, with_neighbours(): after = lax.ppermute(block, axis, [(i + 1, i) for i in range(count - 1)])  16.5 us
    ppermute x2, waiting for transfers between devices, passed_along(): return lax.ppermute(block, axis, route)  14.9 us
    add x14, other arithmetic, on_device(): state = state + 0.5 * (first + second)  7.31 us
    add x14, other arithmetic, on_device(): state + first  7.01 us
    ppermute x1, waiting for transfers between devices, with_neighbours(): before = lax.ppermute(block, axis, [(i, i + 1) for i in range(count - 1)])  6.18 us
    ppermute x1, starting transfers between devices, with_neighbours(): after = lax.ppermute(block, axis, [(i + 1, i) for i in range(count - 1)])  5.1 us
  transfers between devices with their start and end apart: 5, of which 5 were waited for; matrix products, arithmetic and copies ran while one was open for 0% of the time, Pallas kernels for 0%

profile of v1, /device:TPU:16, one launch (start us, length us, event | category | flops | bytes accessed | tf_op | source)
XLA Modules:
  0.0 180.3 jit_solution(16393221735521170525)
XLA Ops:
  6.5 2.7 %pad_maximum_fusion.1 = f32[49,64,128]{2,1,0:T(8,128)} fusion(f32[1,64,128]{2,1,0:T(8,128)} %bitcast.140, f32[32,64,128]{2,1,0:T(8,128)} %bitcast.113, f32[16,64,128]{2,1,0:T(8,128)} %bitcast.124), kind=kLoop, calls=%fused_computation.1 | loop fusion | flops 802816 | bytes 3211264 | tf_op jit(solution)/shard_map/concatenate | solution.py:75
  9.3 5.1 %collective-permute-start.1 = (f32[49,64,128]{2,1,0:T(8,128)}, f32[49,64,128]{2,1,0:T(8,128)S(1)}, u32[]{:S(2)}, u32[]{:S(2)}) collective-permute-start(f32[49,64,128]{2,1,0:T(8,128)} %pad_maximum_fusion.1), channel_id=1, source_target_pairs={{1,0},{2,1},{3,2},{4,3},{5,4},{6,5},{7,6},{8,7},{9,8},{10,9},{11,1... | collective-permute-start | bytes 4816904 | tf_op jit(solution)/shard_map/ppermute | solution.py:24
  14.4 1.9 %collective-permute-start = (f32[49,64,128]{2,1,0:T(8,128)}, f32[49,64,128]{2,1,0:T(8,128)S(1)}, u32[]{:S(2)}, u32[]{:S(2)}) collective-permute-start(f32[49,64,128]{2,1,0:T(8,128)} %pad_maximum_fusion.1), channel_id=1, source_target_pairs={{0,1},{1,2},{2,3},{3,4},{4,5},{5,6},{6,7},{7,8},{8,9},{9,10},{10,1... | collective-permute-start | bytes 4816904 | tf_op jit(solution)/shard_map/ppermute | solution.py:23
  16.5 16.5 %collective-permute-done.1 = f32[49,64,128]{2,1,0:T(8,128)S(1)} collective-permute-done((f32[49,64,128]{2,1,0:T(8,128)}, f32[49,64,128]{2,1,0:T(8,128)S(1)}, u32[]{:S(2)}, u32[]{:S(2)}) %collective-permute-start.1) | collective-permute-done | bytes 1605664 | tf_op jit(solution)/shard_map/ppermute | solution.py:24
  33.0 6.2 %collective-permute-done = f32[49,64,128]{2,1,0:T(8,128)S(1)} collective-permute-done((f32[49,64,128]{2,1,0:T(8,128)}, f32[49,64,128]{2,1,0:T(8,128)S(1)}, u32[]{:S(2)}, u32[]{:S(2)}) %collective-permute-start) | collective-permute-done | bytes 1605664 | tf_op jit(solution)/shard_map/ppermute | solution.py:23
  39.2 1.8 %pad_maximum_fusion = f32[49,192,128]{2,1,0:T(8,128)S(1)} fusion(f32[49,64,128]{2,1,0:T(8,128)S(1)} %collective-permute-done.1, f32[1,64,128]{2,1,0:T(8,128)S(1)} %bitcast.141, f32[32,64,128]{2,1,0:T(8,128)} %bitcast.114, f32[16,64,128]{2,1,0:T(8,128)} %bitcast.125, f32[49,64,128]{2,1,0:T(8,128)S(1)} %collective-permute-done), kind=kLoop, calls=%fused_computation | loop fusion | flops 4816896 | bytes 9633792 | tf_op jit(solution)/shard_map/concatenate | solution.py:25
  41.4 1.0 copy-done
  49.8 1.8 %collective-permute-start.2 = (f32[4,192,128]{2,1,0:T(8,128)S(1)}, f32[4,192,128]{2,1,0:T(8,128)S(1)}, u32[]{:S(2)}, u32[]{:S(2)}) collective-permute-start(f32[4,192,128]{2,1,0:T(8,128)S(1)} %multiply_add_fusion.14), channel_id=1, source_target_pairs={{112,0},{0,16},{16,32},{32,48},{48,64},{64,80},{80,96},{96,112},{1... | collective-permute-start | bytes 1179656 | tf_op jit(solution)/shard_map/ppermute | solution.py:18
  52.0 8.0 %collective-permute-done.2 = f32[4,192,128]{2,1,0:T(8,128)S(1)} collective-permute-done((f32[4,192,128]{2,1,0:T(8,128)S(1)}, f32[4,192,128]{2,1,0:T(8,128)S(1)}, u32[]{:S(2)}, u32[]{:S(2)}) %collective-permute-start.2) | collective-permute-done | bytes 393248 | tf_op jit(solution)/shard_map/ppermute | solution.py:18
  66.5 0.6 broadcast_multiply_fusion.56
  67.7 0.5 broadcast_multiply_fusion.50
  68.3 0.6 broadcast_multiply_fusion.43
  69.5 0.5 broadcast_multiply_fusion.35
  70.6 0.5 broadcast_multiply_fusion.27
  71.8 11.6 %broadcast_multiply_fusion.19 = (f32[4,192,128]{2,1,0:T(8,128)S(1)}, f32[4,192,128]{2,1,0:T(8,128)S(1)}) fusion(f32[192,128]{1,0:T(8,128)S(1)} %get-tuple-element.146, f32[4,192,128]{2,1,0:T(8,128)S(1)} %get-tuple-element.62, f32[4,192,128]{2,1,0:T(8,128)S(1)} %get-tuple-element.60, f32[192]{0:T(256)S(1)} %and_convert_fusion, ...), kind=kLoop, calls=%fused_computation.974 | loop fusion | flops 1966080 | bytes 3343104 | tf_op jit(solution)/shard_map/mul | solution.py:54
  84.0 0.5 broadcast_multiply_fusion.11
  85.2 0.5 broadcast_multiply_fusion.3
  86.4 1.3 fusion.154
  87.6 1.1 collective-permute-start.3
  88.9 6.9 %collective-permute-done.3 = f32[4,192,128]{2,1,0:T(8,128)} collective-permute-done((f32[4,192,128]{2,1,0:T(8,128)}, f32[4,192,128]{2,1,0:T(8,128)}, u32[]{:S(2)}, u32[]{:S(2)}) %collective-permute-start.3) | collective-permute-done | bytes 393248 | tf_op jit(solution)/shard_map/ppermute | solution.py:18
  95.7 1.1 broadcast_multiply_fusion.58
  96.8 2.4 %broadcast_multiply_fusion.54 = (f32[4,192,128]{2,1,0:T(8,128)S(1)}, f32[4,192,128]{2,1,0:T(8,128)S(1)}, f32[4,192,128]{2,1,0:T(8,128)S(1)}) fusion(f32[192,128]{1,0:T(8,128)} %copy-done.27, f32[4,192,128]{2,1,0:T(8,128)} %collective-permute-done.3, f32[192]{0:T(256)S(1)} %and_convert_fusion, f32[192,128]{1,0:T(8,128)S(1)} %get-tuple-element.130, ...), kind=kLoop, calls=%fused_computation.1009 | loop fusion | flops 1769472 | bytes 2949888 | tf_op jit(solution)/shard_map/mul | solution.py:54
  99.3 1.5 broadcast_multiply_fusion.49
  101.8 0.5 broadcast_multiply_fusion.41
  104.8 0.5 broadcast_multiply_fusion.25
  105.9 0.5 broadcast_multiply_fusion.17
  107.4 0.5 broadcast_multiply_fusion.9
  108.8 0.5 broadcast_multiply_fusion.1
  111.1 0.6 copy.10
  111.7 1.8 fusion.509
  113.5 1.7 copy.6
  115.2 58.1 %reduce-scatter.2.cloned.1.call-done = f32[1,2,4,64,128]{4,3,2,1,0:T(8,128)} async-done(((f32[8,2,4,64,128]{4,3,2,1,0:T(8,128)}), f32[1,2,4,64,128]{4,3,2,1,0:T(8,128)}) %reduce-scatter.2.cloned.1.call-update) | async-done | bytes 262160 | tf_op jit(solution)/shard_map/reduce_scatter | solution.py:119
  (153 shorter events, 26.0 us)
Async XLA Ops:
  6.5 32.6 %copy-start.2 = (f32[64,128]{1,0:T(8,128)S(1)}, f32[64,128]{1,0:T(8,128)}, u32[]{:S(2)}) copy-start(f32[64,128]{1,0:T(8,128)} %param.6) | copy-start | bytes 98308
  6.5 166.7 %reduce-scatter.2.cloned.1.call-start = ((), (), s32[]{:S(2)}) async-start(), calls=%async_computation.1 | async-start | bytes 2359296 | tf_op jit(solution)/shard_map/reduce_scatter | solution.py:119
  9.3 23.7 %collective-permute-start.1 = (f32[49,64,128]{2,1,0:T(8,128)}, f32[49,64,128]{2,1,0:T(8,128)S(1)}, u32[]{:S(2)}, u32[]{:S(2)}) collective-permute-start(f32[49,64,128]{2,1,0:T(8,128)} %pad_maximum_fusion.1), channel_id=1, source_target_pairs={{1,0},{2,1},{3,2},{4,3},{5,4},{6,5},{7,6},{8,7},{9,8},{10,9},{11,1... | collective-permute-start | bytes 4816904 | tf_op jit(solution)/shard_map/ppermute | solution.py:24
  14.4 24.8 %collective-permute-start = (f32[49,64,128]{2,1,0:T(8,128)}, f32[49,64,128]{2,1,0:T(8,128)S(1)}, u32[]{:S(2)}, u32[]{:S(2)}) collective-permute-start(f32[49,64,128]{2,1,0:T(8,128)} %pad_maximum_fusion.1), channel_id=1, source_target_pairs={{0,1},{1,2},{2,3},{3,4},{4,5},{5,6},{6,7},{7,8},{8,9},{9,10},{10,1... | collective-permute-start | bytes 4816904 | tf_op jit(solution)/shard_map/ppermute | solution.py:23
  41.1 1.2 copy-start
  41.2 1.3 copy-start.1
  49.8 10.2 %collective-permute-start.2 = (f32[4,192,128]{2,1,0:T(8,128)S(1)}, f32[4,192,128]{2,1,0:T(8,128)S(1)}, u32[]{:S(2)}, u32[]{:S(2)}) collective-permute-start(f32[4,192,128]{2,1,0:T(8,128)S(1)} %multiply_add_fusion.14), channel_id=1, source_target_pairs={{112,0},{0,16},{16,32},{32,48},{48,64},{64,80},{80,96},{96,112},{1... | collective-permute-start | bytes 1179656 | tf_op jit(solution)/shard_map/ppermute | solution.py:18
  51.8 14.6 %copy-start.27 = (f32[192,128]{1,0:T(8,128)}, f32[192,128]{1,0:T(8,128)S(1)}, u32[]{:S(2)}) copy-start(f32[192,128]{1,0:T(8,128)S(1)} %get-tuple-element.136) | copy-start | bytes 294916
  51.9 15.2 %copy-start.25 = (f32[192,128]{1,0:T(8,128)}, f32[192,128]{1,0:T(8,128)S(1)}, u32[]{:S(2)}) copy-start(f32[192,128]{1,0:T(8,128)S(1)} %get-tuple-element.137) | copy-start | bytes 294916
  51.9 15.8 %copy-start.21 = (f32[192,128]{1,0:T(8,128)}, f32[192,128]{1,0:T(8,128)S(1)}, u32[]{:S(2)}) copy-start(f32[192,128]{1,0:T(8,128)S(1)} %get-tuple-element.138) | copy-start | bytes 294916
  51.9 16.4 %copy-start.23 = (f32[192,128]{1,0:T(8,128)}, f32[192,128]{1,0:T(8,128)S(1)}, u32[]{:S(2)}) copy-start(f32[192,128]{1,0:T(8,128)S(1)} %get-tuple-element.139) | copy-start | bytes 294916
  51.9 17.0 %copy-start.7 = (f32[192,128]{1,0:T(8,128)}, f32[192,128]{1,0:T(8,128)S(1)}, u32[]{:S(2)}) copy-start(f32[192,128]{1,0:T(8,128)S(1)} %get-tuple-element.140) | copy-start | bytes 294916
  51.9 17.5 %copy-start.19 = (f32[192,128]{1,0:T(8,128)}, f32[192,128]{1,0:T(8,128)S(1)}, u32[]{:S(2)}) copy-start(f32[192,128]{1,0:T(8,128)S(1)} %get-tuple-element.141) | copy-start | bytes 294916
  51.9 18.1 %copy-start.5 = (f32[192,128]{1,0:T(8,128)}, f32[192,128]{1,0:T(8,128)S(1)}, u32[]{:S(2)}) copy-start(f32[192,128]{1,0:T(8,128)S(1)} %get-tuple-element.142) | copy-start | bytes 294916
  51.9 18.7 %copy-start.17 = (f32[192,128]{1,0:T(8,128)}, f32[192,128]{1,0:T(8,128)S(1)}, u32[]{:S(2)}) copy-start(f32[192,128]{1,0:T(8,128)S(1)} %get-tuple-element.143) | copy-start | bytes 294916
  51.9 19.3 %copy-start.3 = (f32[192,128]{1,0:T(8,128)}, f32[192,128]{1,0:T(8,128)S(1)}, u32[]{:S(2)}) copy-start(f32[192,128]{1,0:T(8,128)S(1)} %get-tuple-element.144) | copy-start | bytes 294916
  51.9 19.8 %copy-start.15 = (f32[192,128]{1,0:T(8,128)}, f32[192,128]{1,0:T(8,128)S(1)}, u32[]{:S(2)}) copy-start(f32[192,128]{1,0:T(8,128)S(1)} %get-tuple-element.145) | copy-start | bytes 294916
  51.9 32.0 %copy-start.13 = (f32[192,128]{1,0:T(8,128)}, f32[192,128]{1,0:T(8,128)S(1)}, u32[]{:S(2)}) copy-start(f32[192,128]{1,0:T(8,128)S(1)} %get-tuple-element.147) | copy-start | bytes 294916
  52.0 33.2 %copy-start.11 = (f32[192,128]{1,0:T(8,128)}, f32[192,128]{1,0:T(8,128)S(1)}, u32[]{:S(2)}) copy-start(f32[192,128]{1,0:T(8,128)S(1)} %get-tuple-element.149) | copy-start | bytes 294916
  52.0 34.3 %copy-start.9 = (f32[192,128]{1,0:T(8,128)}, f32[192,128]{1,0:T(8,128)S(1)}, u32[]{:S(2)}) copy-start(f32[192,128]{1,0:T(8,128)S(1)} %get-tuple-element.135) | copy-start | bytes 294916
  86.3 2.4 %copy-start.28 = (s32[8]{0:T(128)S(1)}, s32[8]{0:T(128)}, u32[]{:S(2)}) copy-start(s32[8]{0:T(128)} %param.7) | copy-start | bytes 100
  87.6 8.1 %collective-permute-start.3 = (f32[4,192,128]{2,1,0:T(8,128)}, f32[4,192,128]{2,1,0:T(8,128)}, u32[]{:S(2)}, u32[]{:S(2)}) collective-permute-start(f32[4,192,128]{2,1,0:T(8,128)} %fusion.154), channel_id=1, source_target_pairs={{16,0},{32,16},{48,32},{64,48},{80,64},{96,80},{112,96},{0,112},{1... | collective-permute-start | bytes 1179656 | tf_op jit(solution)/shard_map/ppermute | solution.py:18
  88.8 10.4 %copy-start.26 = (f32[192,128]{1,0:T(8,128)S(1)}, f32[192,128]{1,0:T(8,128)}, u32[]{:S(2)}) copy-start(f32[192,128]{1,0:T(8,128)} %copy-done.25) | copy-start | bytes 294916
  96.8 2.5 %copy-start.22 = (f32[192,128]{1,0:T(8,128)S(1)}, f32[192,128]{1,0:T(8,128)}, u32[]{:S(2)}) copy-start(f32[192,128]{1,0:T(8,128)} %copy-done.21) | copy-start | bytes 294916
  99.3 1.6 copy-start.24
  100.9 0.9 copy-start.8
  101.4 0.9 copy-start.20
  102.4 0.9 copy-start.6
  102.9 0.9 copy-start.18
  103.9 0.9 copy-start.4
  104.4 0.9 copy-start.16
  105.9 0.9 copy-start.14
  (2 other events, 1.8 us)
Sparse Core Ops, SparseCore 0:
  115.3 57.8 reduce-scatter.1
